TPU v7x, 512 devices: a whole 4x8x8 slice. The times are simulated.
512 devices in a mesh: dp: 32 (over y, x), feat: 16 (over z, core).
Axes of the slice: x: 4, y: 8, z: 8, core: 2. Of those that a mesh axis runs over, the one named last changes fastest.
Arguments:
- tokens: bfloat16 [4096, 8192], P('dp', 'feat'), may hold values from -6 to 6
- targets: bfloat16 [8192, 8192], P('dp', 'feat'), may hold values from -6 to 6
- first_blocks: bfloat16 [128, 64, 256], P('feat'), may hold values from -0.75 to 0.75
- second_factor_blocks: bfloat16 [128, 256, 256], P('feat'), may hold values from -0.375 to 0.375
- down_blocks: bfloat16 [128, 256, 64], P('feat'), may hold values from -0.375 to 0.375
- first_tangent: bfloat16 [128, 64, 256], P('feat'), may hold values from -0.75 to 0.75
- second_factor_tangent: bfloat16 [128, 256, 256], P('feat'), may hold values from -0.375 to 0.375
- doc_lengths: int32 [32, 32], replicated, may hold values from 1 to 8, as said below
- doc_owners: int32 [32, 32], replicated, may hold values from 0 to 31, as said below
- pack_offsets: int32 [32, 32], replicated, may hold values from 0 to 248, as said below
Outputs:
- hess_first: float32 [128, 64, 256], P('feat', 'dp')
- hess_mixed: float32 [128, 256, 256], P('feat', 'dp')
Inputs may be any that keep to these rules, and one draw needn't show every extreme that they name: `doc_lengths`: the 32 lengths of one loader sum to 128; the longest has exactly 8 rows. `doc_owners`: A loader sends exactly one document to each owner; some owner receives exactly 256 rows in all, and none more. `pack_offsets`: each owner's documents lie end to end from row 0 of its pack, in the order of their loaders.
All inputs are finite; a program needn't handle non-finite values.
Results may differ from a plain program's by a relative error of at most 0.0072.
Values may be sent and summed in bfloat16 or wider, within the bound.
No kernel may reach another device: no remote copies, remote signals or barrier semaphores. Data moves between devices by JAX's collectives and lax.ppermute only.
A program may use at most 64 MiB of HBM per device.

v0:
```python
import jax
import jax.numpy as jnp
from jax import lax
from jax.sharding import PartitionSpec as P

inv_root_two = 0.7071067811865476
inv_root_two_pi = 0.3989422804014327


def curvature(
    tok_rows,
    goal_rows,
    weight,
    first_blocks,
    second_factor_blocks,
    down_blocks,
    first_tangent,
    second_factor_tangent,
):
    features = lax.axis_size("feat")
    row_count = tok_rows.shape[0]
    local_blocks, block_in, block_out = first_blocks.shape
    pair_size = block_out // (local_blocks * features)
    token_blocks = tok_rows.reshape(row_count, local_blocks, block_in)
    goal_blocks = goal_rows.reshape(row_count, local_blocks, block_in)
    split_shape = (local_blocks, block_in, features, local_blocks, pair_size)
    down_shape = (local_blocks, features, local_blocks, pair_size, block_in)
    first_act = jnp.einsum(
        "rki,kiGgc->Ggkcr",
        token_blocks,
        first_blocks.reshape(split_shape),
        preferred_element_type=jnp.float32,
    ).astype(jnp.bfloat16)
    tangents = jnp.einsum(
        "rki,kiGgc->Ggkcr",
        token_blocks,
        first_tangent.reshape(split_shape),
        preferred_element_type=jnp.float32,
    ).astype(jnp.bfloat16)
    out_grad = (
        jnp.einsum(
            "rkd,kGgcd->Ggkcr",
            goal_blocks,
            down_blocks.reshape(down_shape),
            preferred_element_type=jnp.float32,
        )
        * weight
    ).astype(jnp.bfloat16)
    stacked = jnp.stack([first_act, tangents, out_grad], axis=1)
    mixed = lax.all_to_all(stacked, "feat", split_axis=0, concat_axis=3, tiled=True)
    hidden_shape = (local_blocks, block_out, row_count)
    mixed_activation = mixed[0, 0].reshape(hidden_shape)
    mixed_tangent_value = mixed[0, 1].reshape(hidden_shape)
    hidden_grad = mixed[0, 2].reshape(hidden_shape)
    pre_act = jnp.einsum(
        "vca,vcf->vfa", mixed_activation, second_factor_blocks, preferred_element_type=jnp.float32
    )
    pre_tan = jnp.einsum(
        "vca,vcf->vfa",
        mixed_tangent_value,
        second_factor_blocks,
        preferred_element_type=jnp.float32,
    ) + jnp.einsum(
        "vca,vcf->vfa", mixed_activation, second_factor_tangent, preferred_element_type=jnp.float32
    )
    density = jnp.exp(-0.5 * pre_act * pre_act) * inv_root_two_pi
    normal_cdf = 0.5 * (1.0 + lax.erf(pre_act * inv_root_two))
    preactivation_gradient = (hidden_grad * (normal_cdf + pre_act * density)).astype(jnp.bfloat16)
    preactivation_tangent_gradient = (
        hidden_grad * (density * (2.0 - pre_act * pre_act)) * pre_tan
    ).astype(jnp.bfloat16)
    hess_mixed = jnp.einsum(
        "evp,eqp->evq",
        mixed_tangent_value,
        preactivation_gradient,
        preferred_element_type=jnp.float32,
    ) + jnp.einsum(
        "evp,eqp->evq",
        mixed_activation,
        preactivation_tangent_gradient,
        preferred_element_type=jnp.float32,
    )
    back_mixed = jnp.einsum(
        "bip,bfi->bfp",
        preactivation_tangent_gradient,
        second_factor_blocks,
        preferred_element_type=jnp.float32,
    ) + jnp.einsum(
        "bip,bfi->bfp",
        preactivation_gradient,
        second_factor_tangent,
        preferred_element_type=jnp.float32,
    )
    back_split = back_mixed.astype(jnp.bfloat16).reshape(
        local_blocks, features, local_blocks, pair_size, row_count
    )
    back_first = lax.all_to_all(back_split, "feat", split_axis=1, concat_axis=0, tiled=True)
    back_first = back_first.reshape(local_blocks * features, local_blocks, pair_size, row_count)
    hess_first = jnp.einsum(
        "gkcr,rki->kigc", back_first, token_blocks, preferred_element_type=jnp.float32
    ).reshape(local_blocks, block_in, block_out)
    return (hess_first, hess_mixed)


def per_device(
    tokens,
    targets,
    first_blocks,
    second_factor_blocks,
    down_blocks,
    first_tangent,
    second_factor_tangent,
    doc_lengths,
    doc_owners,
    pack_offsets,
):
    loaders = lax.axis_size("dp")
    device = lax.axis_index("dp")
    tok_count = tokens.shape[0]
    feature_cols = tokens.shape[1]
    slot_rows = 2 * tok_count // loaders
    position = jnp.arange(slot_rows, dtype=jnp.int32)
    mine = (doc_owners == device).astype(jnp.int32)
    first_row = jnp.sum(mine * pack_offsets, axis=1)
    doc_span = jnp.sum(mine * doc_lengths, axis=1)
    in_slot = position[None, :] < doc_span[:, None]
    source = jnp.where(in_slot, first_row[:, None] + position[None, :], 0)
    outgoing = jnp.take(targets, source.reshape(-1), axis=0).reshape(
        loaders, slot_rows, feature_cols
    )
    arrived = lax.all_to_all(outgoing, "dp", split_axis=0, concat_axis=0, tiled=True)
    my_lengths = lax.dynamic_index_in_dim(doc_lengths, device, 0, keepdims=False)
    my_owners = lax.dynamic_index_in_dim(doc_owners, device, 0, keepdims=False)
    my_starts = jnp.cumsum(my_lengths) - my_lengths
    token_pos = jnp.arange(tok_count, dtype=jnp.int32)
    inside = (token_pos[:, None] >= my_starts[None, :]) & (
        token_pos[:, None] < (my_starts + my_lengths)[None, :]
    )
    inside_int = inside.astype(jnp.int32)
    goal_index = (
        jnp.sum(inside_int * (my_owners * slot_rows - my_starts)[None, :], axis=1) + token_pos
    )
    weight = jnp.sum(inside.astype(jnp.float32) / my_lengths.astype(jnp.float32)[None, :], axis=1)
    goal_rows = jnp.take(arrived.reshape(loaders * slot_rows, feature_cols), goal_index, axis=0)
    hess_first, hess_mixed = curvature(
        tokens,
        goal_rows,
        weight,
        first_blocks,
        second_factor_blocks,
        down_blocks,
        first_tangent,
        second_factor_tangent,
    )
    local_blocks = hess_first.shape[0]
    first_part = hess_first.reshape(local_blocks, loaders, -1)
    mixed_part = hess_mixed.reshape(local_blocks, loaders, -1)
    first_width = first_part.shape[2]
    partials = jnp.concatenate([first_part, mixed_part], axis=2)
    gathered = lax.all_to_all(partials, "dp", split_axis=1, concat_axis=1, tiled=True)
    total = jnp.sum(gathered, axis=1)
    hess_first = total[:, :first_width].reshape(local_blocks, -1, hess_first.shape[2])
    hess_mixed = total[:, first_width:].reshape(local_blocks, -1, hess_mixed.shape[2])
    return (hess_first, hess_mixed)


def solution(mesh):
    in_specs = (
        P("dp", "feat"),
        P("dp", "feat"),
        P("feat", None, None),
        P("feat", None, None),
        P("feat", None, None),
        P("feat", None, None),
        P("feat", None, None),
        P(),
        P(),
        P(),
    )
    out_specs = (P("feat", "dp", None), P("feat", "dp", None))
    return jax.shard_map(
        per_device, mesh=mesh, in_specs=in_specs, out_specs=out_specs, check_vma=False
    )
```

profile of v0, /device:TPU:1, one launch (start us, length us, event | category | flops | bytes accessed | tf_op | source)
XLA Modules:
  0.0 198.2 jit_solution(6791670290175771214)
XLA Ops:
  0.7 1.0 select_reduce_fusion.1
  2.0 2.3 %gather_fusion = bf16[256,512]{1,0:T(8,128)(2,1)S(1)} fusion(bf16[256,512]{1,0:T(8,128)(2,1)} %param.11, s32[1024]{0:T(1024)S(1)} %pad_clamp_fusion.1), kind=kCustom, calls=%fused_computation | custom fusion | bytes 525312 | tf_op jit(solution)/shard_map/jit(_take)/gather | solution.py:128
  4.2 0.8 bitcast_select_fusion
  5.0 10.5 %all-to-all-start = ((bf16[32,8,512]{2,1,0:T(8,128)(2,1)}), bf16[32,8,512]{2,1,0:T(8,128)(2,1)S(1)}, u32[]{:S(2)}, u32[]{:S(2)}) async-start(bf16[32,8,512]{2,1,0:T(8,128)(2,1)} %bitcast_select_fusion), calls=%async_computation | async-start | bytes 524288 | tf_op jit(solution)/shard_map/all_to_all | solution.py:131
  15.5 0.7 fusion.38
  16.5 0.7 subtract_bitcast_fusion
  17.9 1.1 copy.89
  19.9 7.0 %all-to-all-done = bf16[32,8,512]{2,1,0:T(8,128)(2,1)S(1)} async-done(((bf16[32,8,512]{2,1,0:T(8,128)(2,1)}), bf16[32,8,512]{2,1,0:T(8,128)(2,1)S(1)}, u32[]{:S(2)}, u32[]{:S(2)}) %all-to-all-start) | async-done | bytes 262176 | tf_op jit(solution)/shard_map/all_to_all | solution.py:131
  26.8 0.8 gather_fusion.1
  27.8 1.3 fusion.5
  29.8 52.3 %all_to_all.43 = bf16[16,3,8,8,2,128]{5,2,4,3,1,0:T(8,128)(2,1)S(1)} all-to-all(bf16[16,3,8,8,2,128]{5,2,4,3,1,0:T(8,128)(2,1)S(1)} %copy.92), channel_id=1, replica_groups=mesh['dp'=32,'feat'=16] {'feat'}, dimensions={0} | all-to-all | bytes 3145728 | tf_op jit(solution)/shard_map/all_to_all | solution.py:50
  83.3 1.6 copy.94
  84.9 1.6 copy.97
  86.9 0.9 fusion.16
  88.1 0.6 fusion.4
  88.7 0.8 copy-done.3
  89.5 0.5 fusion.40
  90.0 0.5 fusion.8
  90.5 1.1 copy.102
  91.6 4.3 %all-to-all-start.2 = ((bf16[8,16,8,2,128]{4,0,3,2,1:T(8,128)(2,1)}), bf16[8,16,8,2,128]{4,0,3,2,1:T(8,128)(2,1)}, u32[]{:S(2)}, u32[]{:S(2)}) async-start(bf16[8,16,8,2,128]{4,0,3,2,1:T(8,128)(2,1)} %bitcast.37), calls=%async_computation.2 | async-start | bytes 1048576 | tf_op jit(solution)/shard_map/all_to_all | solution.py:97
  96.4 0.6 copy-done.2
  97.6 1.5 reshape.162
  99.1 2.8 %copy.110 = f32[8,32,2048]{2,0,1:T(8,128)S(1)} copy(f32[8,32,2048]{2,1,0:T(8,128)} %reshape.162) | data formatting | bytes 4194304 | tf_op jit(solution)/shard_map/reshape | solution.py:157
  101.9 9.7 %all-to-all-done.2 = bf16[8,16,8,2,128]{4,0,3,2,1:T(8,128)(2,1)} async-done(((bf16[8,16,8,2,128]{4,0,3,2,1:T(8,128)(2,1)}), bf16[8,16,8,2,128]{4,0,3,2,1:T(8,128)(2,1)}, u32[]{:S(2)}, u32[]{:S(2)}) %all-to-all-start.2) | async-done | bytes 524320 | tf_op jit(solution)/shard_map/all_to_all | solution.py:97
  111.6 2.2 %convolution_bitcast_fusion.1 = f32[8,64,128,2]{2,1,3,0:T(8,128)} fusion(bf16[128,8,64,1]{0,2,3,1:T(8,128)(2,1)S(1)} %bitcast.114, bf16[8,16,8,2,128]{4,0,3,2,1:T(8,128)(2,1)} %all-to-all-done.2), kind=kOutput, calls=%fused_computation.22 | convolution fusion | flops 33554432 | bytes 1179648 | tf_op jit(solution)/shard_map/gkcr,rki->kigc/dot_general | solution.py:99
  113.8 7.1 %copy.104 = f32[8,64,128,2]{0,3,2,1:T(2,128)} copy(f32[8,64,128,2]{2,1,3,0:T(8,128)} %convolution_bitcast_fusion.1) | data formatting | bytes 1048576 | tf_op jit(solution)/shard_map/gkcr,rki->kigc/dot_general | solution.py:99
  120.9 5.8 %copy.109 = f32[8,32,512]{2,0,1:T(8,128)} copy(f32[8,32,512]{0,2,1:T(8,128)} %bitcast.103) | data formatting | bytes 1048576 | tf_op jit(solution)/shard_map/reshape;reshape | solution.py:156
  126.7 1.2 pad_maximum_fusion
  128.0 67.1 %all_to_all.44 = f32[8,32,2560]{2,0,1:T(8,128)} all-to-all(f32[8,32,2560]{2,0,1:T(8,128)S(1)} %pad_maximum_fusion), channel_id=1, replica_groups=mesh['dp'=32,'feat'=16] {'dp'}, dimensions={1} | all-to-all | bytes 5242880 | tf_op jit(solution)/shard_map/all_to_all | solution.py:160
  195.1 1.9 reduce_sum.52
  197.0 0.7 copy.145
  197.6 0.6 reshape.163
  (52 shorter events, 5.7 us)
Async XLA Ops:
  0.6 85.9 %copy-start = (bf16[8,256,256]{2,1,0:T(8,128)(2,1)S(1)}, bf16[8,256,256]{2,1,0:T(8,128)(2,1)}, u32[]{:S(2)}) copy-start(bf16[8,256,256]{2,1,0:T(8,128)(2,1)} %param.13) | copy-start | bytes 3145732
  0.6 16.8 %copy-start.11 = (bf16[128,512]{1,0:T(8,128)(2,1)S(1)}, bf16[128,512]{1,0:T(8,128)(2,1)}, u32[]{:S(2)}) copy-start(bf16[128,512]{1,0:T(8,128)(2,1)} %param.10) | copy-start | bytes 393220
  0.7 16.9 %copy-start.8 = (bf16[8,64,256]{2,1,0:T(8,128)(2,1)S(1)}, bf16[8,64,256]{2,1,0:T(8,128)(2,1)}, u32[]{:S(2)}) copy-start(bf16[8,64,256]{2,1,0:T(8,128)(2,1)} %param.12) | copy-start | bytes 786436
  1.9 15.9 %copy-start.9 = (bf16[8,256,64]{1,2,0:T(8,128)(2,1)S(1)}, bf16[8,256,64]{1,2,0:T(8,128)(2,1)}, u32[]{:S(2)}) copy-start(bf16[8,256,64]{1,2,0:T(8,128)(2,1)} %param.14) | copy-start | bytes 786436
  1.9 17.0 %copy-start.10 = (bf16[8,64,256]{2,1,0:T(8,128)(2,1)S(1)}, bf16[8,64,256]{2,1,0:T(8,128)(2,1)}, u32[]{:S(2)}) copy-start(bf16[8,64,256]{2,1,0:T(8,128)(2,1)} %param.15) | copy-start | bytes 786436
  5.0 21.8 %all-to-all-start = ((bf16[32,8,512]{2,1,0:T(8,128)(2,1)}), bf16[32,8,512]{2,1,0:T(8,128)(2,1)S(1)}, u32[]{:S(2)}, u32[]{:S(2)}) async-start(bf16[32,8,512]{2,1,0:T(8,128)(2,1)} %bitcast_select_fusion), calls=%async_computation | async-start | bytes 524288 | tf_op jit(solution)/shard_map/all_to_all | solution.py:131
  83.3 4.5 %copy-start.1 = (bf16[1,1,8,128,2,128]{5,2,4,3,1,0:T(8,128)(2,1)}, bf16[1,1,8,128,2,128]{5,2,4,3,1,0:T(8,128)(2,1)S(1)}, u32[]{:S(2)}) copy-start(bf16[1,1,8,128,2,128]{5,2,4,3,1,0:T(8,128)(2,1)S(1)} %copy.95) | copy-start | bytes 1572868
  86.9 1.2 copy-start.7
  87.8 2.2 %copy-start.5 = (bf16[8,256,128]{1,2,0:T(8,128)(2,1)}, bf16[8,256,128]{1,2,0:T(8,128)(2,1)S(1)}, u32[]{:S(2)}) copy-start(bf16[8,256,128]{1,2,0:T(8,128)(2,1)S(1)} %get-tuple-element.10) | copy-start | bytes 1572868
  88.7 0.8 copy-start.3
  90.5 5.4 %copy-start.6 = (bf16[8,256,128]{1,2,0:T(8,128)(2,1)S(1)}, bf16[8,256,128]{1,2,0:T(8,128)(2,1)}, u32[]{:S(2)}) copy-start(bf16[8,256,128]{1,2,0:T(8,128)(2,1)} %copy-done.5) | copy-start | bytes 1572868
  91.6 20.0 %all-to-all-start.2 = ((bf16[8,16,8,2,128]{4,0,3,2,1:T(8,128)(2,1)}), bf16[8,16,8,2,128]{4,0,3,2,1:T(8,128)(2,1)}, u32[]{:S(2)}, u32[]{:S(2)}) async-start(bf16[8,16,8,2,128]{4,0,3,2,1:T(8,128)(2,1)} %bitcast.37), calls=%async_computation.2 | async-start | bytes 1048576 | tf_op jit(solution)/shard_map/all_to_all | solution.py:97
  95.9 1.0 copy-start.2
  96.0 1.2 copy-start.4
where the time goes:
time: 199 us; the launch traced here: 198 us
  blocking collectives  119 us (60%)
  local copies, waits for them, and re-layouts  32.2 us (16%)
  waiting for transfers between devices  16.6 us (8%)
  starting transfers between devices  14.8 us (7%)
  matrix products  7.74 us (4%)
  other arithmetic  6.5 us (3%)
    all_to_all x1, blocking collectives, per_device(): lax.all_to_all(partials, 'dp', split_axis=1, concat_axis=1, tiled=True)  67.1 us
    all_to_all x1, blocking collectives, curvature(): lax.all_to_all(stacked, 'feat', split_axis=0, concat_axis=3, tiled=True)  52.3 us
    all_to_all x1, starting transfers between devices, per_device(): lax.all_to_all(outgoing, 'dp', split_axis=0, concat_axis=0, tiled=True)  10.5 us
    all_to_all x1, waiting for transfers between devices, curvature(): lax.all_to_all(back_split, 'feat', split_axis=1, concat_axis=0, tiled=True)  9.69 us
    dot_general x1, local copies, waits for them, and re-layouts, curvature(): jnp.einsum('gkcr,rki->kigc', back_first, token_blocks, preferred_element_...  7.09 us
    all_to_all x1, waiting for transfers between devices, per_device(): lax.all_to_all(outgoing, 'dp', split_axis=0, concat_axis=0, tiled=True)  6.95 us
    another operation x1, local copies, waits for them, and re-layouts, per_device(): first_part = hess_first.reshape(local_blocks, loaders, -1)  5.85 us
    unnamed x29, local copies, waits for them, and re-layouts  4.36 us
  transfers between devices with their start and end apart: 2, of which 2 were waited for; matrix products, arithmetic and copies ran while one was open for 5% of the time, Pallas kernels for 0%

commit v1 on v0

--- a/solution.py
+++ b/solution.py
@@ -157,7 +157,10 @@
     mixed_part = hess_mixed.reshape(local_blocks, loaders, -1)
     first_width = first_part.shape[2]
     partials = jnp.concatenate([first_part, mixed_part], axis=2)
-    gathered = lax.all_to_all(partials, "dp", split_axis=1, concat_axis=1, tiled=True)
+    gathered = jnp.concatenate(
+        lax.all_to_all(jnp.stack(jnp.split(partials, lax.axis_size("dp"), axis=1)), "dp", 0, 0),
+        axis=1,
+    )
     total = jnp.sum(gathered, axis=1)
     hess_first = total[:, :first_width].reshape(local_blocks, -1, hess_first.shape[2])
     hess_mixed = total[:, first_width:].reshape(local_blocks, -1, hess_mixed.shape[2])

time: 199 us -> 203 us (1.020)
  local copies, waits for them, and re-layouts: 32.2 us -> 28.1 us
  other arithmetic: 6.5 us -> 10.3 us
  matrix products: 7.74 us -> 10.2 us
    unnamed x0 -> x31, other arithmetic: none -> 3.39 us
    reshape x2 -> x1, local copies, waits for them, and re-layouts: 4.34 us -> 1.71 us  [per_device(): mixed_part = hess_mixed.reshape(local_blocks, loaders, -1)]
    unnamed x29 -> x25, local copies, waits for them, and re-layouts: 4.36 us -> 2.88 us
where the time goes in v1:
time: 203 us; the launch traced here: 201 us
  blocking collectives  119 us (59%)
  local copies, waits for them, and re-layouts  28.1 us (14%)
  waiting for transfers between devices  17.6 us (9%)
  starting transfers between devices  14.8 us (7%)
  other arithmetic  10.3 us (5%)
  matrix products  10.2 us (5%)
    all_to_all x1, blocking collectives, per_device(): lax.all_to_all(jnp.stack(jnp.split(partials, lax.axis_size('dp'), axis=1)...  67 us
    all_to_all x1, blocking collectives, curvature(): lax.all_to_all(stacked, 'feat', split_axis=0, concat_axis=3, tiled=True)  52.3 us
    all_to_all x1, waiting for transfers between devices, curvature(): lax.all_to_all(back_split, 'feat', split_axis=1, concat_axis=0, tiled=True)  10.7 us
    all_to_all x1, starting transfers between devices, per_device(): lax.all_to_all(outgoing, 'dp', split_axis=0, concat_axis=0, tiled=True)  10.5 us
    dot_general x1, local copies, waits for them, and re-layouts, curvature(): jnp.einsum('gkcr,rki->kigc', back_first, token_blocks, preferred_element_...  7.09 us
    all_to_all x1, waiting for transfers between devices, per_device(): lax.all_to_all(outgoing, 'dp', split_axis=0, concat_axis=0, tiled=True)  6.94 us
    another operation x1, local copies, waits for them, and re-layouts, per_device(): first_part = hess_first.reshape(local_blocks, loaders, -1)  5.87 us
    all_to_all x1, starting transfers between devices, curvature(): lax.all_to_all(back_split, 'feat', split_axis=1, concat_axis=0, tiled=True)  4.32 us
  transfers between devices with their start and end apart: 2, of which 2 were waited for; matrix products, arithmetic and copies ran while one was open for 5% of the time, Pallas kernels for 0%

profile of v1, /device:TPU:1, one launch (start us, length us, event | category | flops | bytes accessed | tf_op | source)
XLA Modules:
  0.0 201.5 jit_solution(17625875082988256325)
XLA Ops:
  0.7 1.0 select_reduce_fusion.1
  2.0 2.2 %gather_fusion = bf16[256,512]{1,0:T(8,128)(2,1)S(1)} fusion(bf16[256,512]{1,0:T(8,128)(2,1)} %param.11, s32[1024]{0:T(1024)S(1)} %pad_clamp_fusion.1), kind=kCustom, calls=%fused_computation | custom fusion | bytes 525312 | tf_op jit(solution)/shard_map/jit(_take)/gather | solution.py:128
  4.2 0.8 bitcast_select_fusion
  5.0 10.5 %all-to-all-start = ((bf16[32,8,512]{2,1,0:T(8,128)(2,1)}), bf16[32,8,512]{2,1,0:T(8,128)(2,1)S(1)}, u32[]{:S(2)}, u32[]{:S(2)}) async-start(bf16[32,8,512]{2,1,0:T(8,128)(2,1)} %bitcast_select_fusion), calls=%async_computation | async-start | bytes 524288 | tf_op jit(solution)/shard_map/all_to_all | solution.py:131
  15.5 0.7 fusion.71
  16.5 0.7 subtract_bitcast_fusion
  17.9 1.1 copy.88
  19.9 6.9 %all-to-all-done = bf16[32,8,512]{2,1,0:T(8,128)(2,1)S(1)} async-done(((bf16[32,8,512]{2,1,0:T(8,128)(2,1)}), bf16[32,8,512]{2,1,0:T(8,128)(2,1)S(1)}, u32[]{:S(2)}, u32[]{:S(2)}) %all-to-all-start) | async-done | bytes 262176 | tf_op jit(solution)/shard_map/all_to_all | solution.py:131
  26.8 0.8 gather_fusion.1
  27.8 1.3 fusion.5
  29.3 0.4 copy.91
  29.8 52.3 %all_to_all.43 = bf16[16,3,8,8,2,128]{5,2,4,3,1,0:T(8,128)(2,1)S(1)} all-to-all(bf16[16,3,8,8,2,128]{5,2,4,3,1,0:T(8,128)(2,1)S(1)} %copy.91), channel_id=1, replica_groups=mesh['dp'=32,'feat'=16] {'feat'}, dimensions={0} | all-to-all | bytes 3145728 | tf_op jit(solution)/shard_map/all_to_all | solution.py:50
  83.3 1.6 copy.93
  84.9 1.6 copy.96
  86.9 0.9 fusion.16
  88.1 0.6 fusion.4
  88.7 0.5 fusion.73
  89.2 0.5 fusion.8
  89.7 1.1 copy.101
  90.8 4.3 %all-to-all-start.2 = ((bf16[8,16,8,2,128]{4,0,3,2,1:T(8,128)(2,1)}), bf16[8,16,8,2,128]{4,0,3,2,1:T(8,128)(2,1)}, u32[]{:S(2)}, u32[]{:S(2)}) async-start(bf16[8,16,8,2,128]{4,0,3,2,1:T(8,128)(2,1)} %bitcast.37), calls=%async_computation.2 | async-start | bytes 1048576 | tf_op jit(solution)/shard_map/all_to_all | solution.py:97
  95.1 1.5 fusion.24
  96.6 1.8 convolution_add_fusion
  98.4 1.7 reshape.164
  100.1 10.7 %all-to-all-done.2 = bf16[8,16,8,2,128]{4,0,3,2,1:T(8,128)(2,1)} async-done(((bf16[8,16,8,2,128]{4,0,3,2,1:T(8,128)(2,1)}), bf16[8,16,8,2,128]{4,0,3,2,1:T(8,128)(2,1)}, u32[]{:S(2)}, u32[]{:S(2)}) %all-to-all-start.2) | async-done | bytes 524320 | tf_op jit(solution)/shard_map/all_to_all | solution.py:97
  110.8 2.2 %convolution_bitcast_fusion.1 = f32[8,64,128,2]{2,1,3,0:T(8,128)} fusion(bf16[128,8,64,1]{0,2,3,1:T(8,128)(2,1)S(1)} %bitcast.180, bf16[8,16,8,2,128]{4,0,3,2,1:T(8,128)(2,1)} %all-to-all-done.2), kind=kOutput, calls=%fused_computation.83 | convolution fusion | flops 33554432 | bytes 1179648 | tf_op jit(solution)/shard_map/gkcr,rki->kigc/dot_general | solution.py:99
  113.0 7.1 %copy.103 = f32[8,64,128,2]{0,3,2,1:T(2,128)} copy(f32[8,64,128,2]{2,1,3,0:T(8,128)} %convolution_bitcast_fusion.1) | data formatting | bytes 1048576 | tf_op jit(solution)/shard_map/gkcr,rki->kigc/dot_general | solution.py:99
  120.1 5.9 %copy.108 = f32[8,32,512]{2,1,0:T(8,128)} copy(f32[8,32,512]{0,2,1:T(8,128)} %bitcast.169) | data formatting | bytes 1048576 | tf_op jit(solution)/shard_map/reshape;reshape | solution.py:156
  126.0 1.0 bitcast_dynamic-update-slice_fusion.30
  129.7 67.0 %all_to_all.44 = f32[32,8,1,2560]{3,2,1,0:T(1,128)} all-to-all(f32[32,8,1,2560]{3,2,1,0:T(1,128)S(1)} %fusion.64), channel_id=1, replica_groups=mesh['dp'=32,'feat'=16] {'dp'}, dimensions={0} | all-to-all | bytes 5242880 | tf_op jit(solution)/shard_map/all_to_all | solution.py:161
  196.7 3.4 %reduce_sum.52 = f32[8,2560]{1,0:T(8,128)S(1)} reduce(f32[32,8,1,2560]{3,2,1,0:T(1,128)} %all_to_all.44, f32[]{:T(128)} %constant.57.clone.1), dimensions={0,2}, to_apply=%region_5.6 | reduce | flops 634880 | bytes 2703364 | tf_op jit(solution)/shard_map/reduce_sum | solution.py:164
  200.2 0.7 copy.143
  200.9 0.6 reshape.165
  (78 shorter events, 6.9 us)
Async XLA Ops:
  0.6 85.9 %copy-start = (bf16[8,256,256]{2,1,0:T(8,128)(2,1)S(1)}, bf16[8,256,256]{2,1,0:T(8,128)(2,1)}, u32[]{:S(2)}) copy-start(bf16[8,256,256]{2,1,0:T(8,128)(2,1)} %param.13) | copy-start | bytes 3145732
  0.6 16.8 %copy-start.9 = (bf16[128,512]{1,0:T(8,128)(2,1)S(1)}, bf16[128,512]{1,0:T(8,128)(2,1)}, u32[]{:S(2)}) copy-start(bf16[128,512]{1,0:T(8,128)(2,1)} %param.10) | copy-start | bytes 393220
  0.7 16.9 %copy-start.6 = (bf16[8,64,256]{2,1,0:T(8,128)(2,1)S(1)}, bf16[8,64,256]{2,1,0:T(8,128)(2,1)}, u32[]{:S(2)}) copy-start(bf16[8,64,256]{2,1,0:T(8,128)(2,1)} %param.12) | copy-start | bytes 786436
  0.7 17.2 %copy-start.7 = (bf16[8,256,64]{1,2,0:T(8,128)(2,1)S(1)}, bf16[8,256,64]{1,2,0:T(8,128)(2,1)}, u32[]{:S(2)}) copy-start(bf16[8,256,64]{1,2,0:T(8,128)(2,1)} %param.14) | copy-start | bytes 786436
  2.0 17.0 %copy-start.8 = (bf16[8,64,256]{2,1,0:T(8,128)(2,1)S(1)}, bf16[8,64,256]{2,1,0:T(8,128)(2,1)}, u32[]{:S(2)}) copy-start(bf16[8,64,256]{2,1,0:T(8,128)(2,1)} %param.15) | copy-start | bytes 786436
  5.0 21.8 %all-to-all-start = ((bf16[32,8,512]{2,1,0:T(8,128)(2,1)}), bf16[32,8,512]{2,1,0:T(8,128)(2,1)S(1)}, u32[]{:S(2)}, u32[]{:S(2)}) async-start(bf16[32,8,512]{2,1,0:T(8,128)(2,1)} %bitcast_select_fusion), calls=%async_computation | async-start | bytes 524288 | tf_op jit(solution)/shard_map/all_to_all | solution.py:131
  83.0 3.5 %copy-start.2 = (bf16[1,1,8,128,2,128]{5,2,4,3,1,0:T(8,128)(2,1)}, bf16[1,1,8,128,2,128]{5,2,4,3,1,0:T(8,128)(2,1)S(1)}, u32[]{:S(2)}) copy-start(bf16[1,1,8,128,2,128]{5,2,4,3,1,0:T(8,128)(2,1)S(1)} %copy.97) | copy-start | bytes 1572868
  86.9 1.2 copy-start.5
  87.8 1.4 copy-start.4
  89.2 5.9 %copy-start.3 = (bf16[1,1,8,128,2,128]{5,2,4,3,1,0:T(8,128)(2,1)S(1)}, bf16[1,1,8,128,2,128]{5,2,4,3,1,0:T(8,128)(2,1)}, u32[]{:S(2)}) copy-start(bf16[1,1,8,128,2,128]{5,2,4,3,1,0:T(8,128)(2,1)} %copy-done.2) | copy-start | bytes 1572868
  90.8 20.0 %all-to-all-start.2 = ((bf16[8,16,8,2,128]{4,0,3,2,1:T(8,128)(2,1)}), bf16[8,16,8,2,128]{4,0,3,2,1:T(8,128)(2,1)}, u32[]{:S(2)}, u32[]{:S(2)}) async-start(bf16[8,16,8,2,128]{4,0,3,2,1:T(8,128)(2,1)} %bitcast.37), calls=%async_computation.2 | async-start | bytes 1048576 | tf_op jit(solution)/shard_map/all_to_all | solution.py:97
  126.0 1.1 copy-start.1
